TPU v7x, 32 devices: a whole 2x2x4 slice. The times are simulated.
32 devices in a mesh: real: 2 (over x), los: 8 (over z, y), sky: 2 (over core).
Axes of the slice: x: 2, y: 2, z: 4, core: 2. Of those that a mesh axis runs over, the one named last changes fastest.
Arguments:
- density: float32 [16, 2048, 2048], P(('real', 'los'), 'sky'), parts along dimension 0, may hold values from -6 to 8
- lens_weight: float32 [16], P(('real', 'los')), parts along dimension 0, may hold values from 0.05 to 0.4
- plane_count: int32 [16], P(('real', 'los')), parts along dimension 0, may hold values from 0 to 1
- ray_state: float32 [16, 12, 32, 2048], P(('real', 'los'), None, 'sky'), parts along dimension 0, may hold values from -6 to 6
Outputs:
- ray_out: float32 [16, 12, 32, 2048], P(('real', 'los'), None, 'sky'), parts along dimension 0
There are 2 independent parts, one for each index of `real`. A program takes and returns all parts, laid end to end along the dimension named above; each array names one. Nothing has to cross between parts.
All inputs are finite; a program needn't handle non-finite values.
Results may differ from a plain program's by a relative error of at most 0.00012.
Values sent between devices are 32-bit elements; how exact they have to be, the bound alone decides.
No kernel may reach another device: no remote copies, remote signals or barrier semaphores. Data moves between devices by JAX's collectives and lax.ppermute only.
A program may use at most 128 MiB of HBM per device.

v0:
```python
import math
import jax
import jax.numpy as jnp
from jax import lax
from jax.sharding import PartitionSpec as P

HOPS = 4
two_pi = 2.0 * math.pi
highest = lax.Precision.HIGH
first_radix = 16


def shifted(block, axis, distance):
    devices = range(lax.axis_size(axis))
    route = [((i - distance) % len(devices), i) for i in devices]
    return lax.ppermute(block, axis, route)


def lens_step(ray_tile, fields):
    disp_x = ray_tile[..., 0, :, :]
    disp_y = ray_tile[..., 1, :, :]
    tilt_x = ray_tile[..., 2, :, :]
    tilt_y = ray_tile[..., 3, :, :]
    jac_xx = ray_tile[..., 4, :, :]
    jac_xy = ray_tile[..., 5, :, :]
    jac_yx = ray_tile[..., 6, :, :]
    jac_yy = ray_tile[..., 7, :, :]
    rate_xx = ray_tile[..., 8, :, :]
    rate_xy = ray_tile[..., 9, :, :]
    rate_yx = ray_tile[..., 10, :, :]
    rate_yy = ray_tile[..., 11, :, :]
    bend_x = fields[..., 0, :, :]
    bend_y = fields[..., 1, :, :]
    hess_xx = fields[..., 2, :, :]
    hess_yy = fields[..., 3, :, :]
    hess_xy = fields[..., 4, :, :]
    push_x = bend_x + hess_xx * disp_x + hess_xy * disp_y
    push_y = bend_y + hess_xy * disp_x + hess_yy * disp_y
    new_tilt_x = tilt_x - push_x
    new_tilt_y = tilt_y - push_y
    new_disp_x = disp_x + new_tilt_x
    new_disp_y = disp_y + new_tilt_y
    new_rate_xx = rate_xx - (hess_xx * jac_xx + hess_xy * jac_yx)
    new_rate_xy = rate_xy - (hess_xx * jac_xy + hess_xy * jac_yy)
    new_rate_yx = rate_yx - (hess_xy * jac_xx + hess_yy * jac_yx)
    new_rate_yy = rate_yy - (hess_xy * jac_xy + hess_yy * jac_yy)
    new_jac_xx = jac_xx + new_rate_xx
    new_jac_xy = jac_xy + new_rate_xy
    new_jac_yx = jac_yx + new_rate_yx
    new_jac_yy = jac_yy + new_rate_yy
    return jnp.stack(
        [
            new_disp_x,
            new_disp_y,
            new_tilt_x,
            new_tilt_y,
            new_jac_xx,
            new_jac_xy,
            new_jac_yx,
            new_jac_yy,
            new_rate_xx,
            new_rate_xy,
            new_rate_yx,
            new_rate_yy,
        ],
        axis=-3,
    )


def phase_table(left_idx, right_idx, modulus, orient):
    product = left_idx[:, None] * right_idx[None, :] % modulus
    angle = orient * two_pi / modulus * product.astype(jnp.float32)
    return (jnp.cos(angle), jnp.sin(angle))


def block_table(left_idx, right_idx, modulus, orient):
    t_re, t_im = phase_table(left_idx, right_idx, modulus, orient)
    top = jnp.concatenate([t_re, t_im], axis=1)
    bottom = jnp.concatenate([-t_im, t_re], axis=1)
    return jnp.concatenate([top, bottom], axis=0)


def mixed(form, left_op, right_op):
    return jnp.einsum(
        form, left_op, right_op, precision=highest, preferred_element_type=jnp.float32
    )


def complex_product(form, real_in, imag_in, table_re, table_im):
    if imag_in is None:
        return (mixed(form, real_in, table_re), mixed(form, real_in, table_im))
    out_re = mixed(form, real_in, table_re) - mixed(form, imag_in, table_im)
    out_im = mixed(form, real_in, table_im) + mixed(form, imag_in, table_re)
    return (out_re, out_im)


def first_factor_of(length):
    factor_one = 1
    while factor_one * factor_one < length and length % (factor_one * 2) == 0:
        factor_one = factor_one * 2
    return factor_one


def rows_forward(cells):
    row_count, length = cells.shape
    second = length // first_radix
    half = second // 2
    shaped = cells.reshape(row_count, first_radix, second)
    v_idx = jnp.arange(first_radix, dtype=jnp.int32)
    u_idx = jnp.arange(second, dtype=jnp.int32)
    m_idx = jnp.arange(half, dtype=jnp.int32)
    section_re, section_im = phase_table(v_idx, v_idx, first_radix, -1.0)
    part_re = mixed("rvu,vk->rku", shaped, section_re)
    part_im = mixed("rvu,vk->rku", shaped, section_im)
    twist_re, twist_im = phase_table(v_idx, u_idx, length, -1.0)
    turned_re = part_re * twist_re - part_im * twist_im
    turned_im = part_re * twist_im + part_im * twist_re
    final = block_table(u_idx, m_idx, second, -1.0)
    return mixed("rkj,jn->rkn", turned_re, final[:second]) + mixed(
        "rkj,jn->rkn", turned_im, final[second:]
    )


def columns_forward(spread_re, spread_im):
    length, col_count = spread_re.shape
    factor_one = first_factor_of(length)
    second = length // factor_one
    first_idx = jnp.arange(factor_one, dtype=jnp.int32)
    second_idx = jnp.arange(second, dtype=jnp.int32)
    section = block_table(first_idx, first_idx, factor_one, -1.0)
    part = mixed(
        "jn,jbc->nbc", section[:factor_one], spread_re.reshape(factor_one, second, col_count)
    ) + mixed("jn,jbc->nbc", section[factor_one:], spread_im.reshape(factor_one, second, col_count))
    part = part.reshape(2, factor_one, second, col_count)
    twist_re, twist_im = phase_table(first_idx, second_idx, length, -1.0)
    twist_re = twist_re[:, :, None]
    twist_im = twist_im[:, :, None]
    turned_re = part[0] * twist_re - part[1] * twist_im
    turned_im = part[0] * twist_im + part[1] * twist_re
    turned = jnp.stack([turned_re, turned_im], axis=1).reshape(factor_one, 2 * second, col_count)
    final = block_table(second_idx, second_idx, second, -1.0)
    done = mixed("kjc,jn->knc", turned, final)
    return done.reshape(factor_one, 2, second, col_count)


def rows_inverse(spec_re, spec_im, length, m_count):
    row_count = spec_re.shape[0]
    second = length // first_radix
    shaped_re = spec_re.reshape(row_count, first_radix, m_count)
    shaped_im = spec_im.reshape(row_count, first_radix, m_count)
    k_idx = jnp.arange(first_radix, dtype=jnp.int32)
    u_idx = jnp.arange(second, dtype=jnp.int32)
    m_idx = jnp.arange(m_count, dtype=jnp.int32)
    section_re, section_im = phase_table(m_idx, u_idx, second, 1.0)
    part_re, part_im = complex_product("rkm,mu->rku", shaped_re, shaped_im, section_re, section_im)
    twist_re, twist_im = phase_table(k_idx, u_idx, length, 1.0)
    turned_re = part_re * twist_re - part_im * twist_im
    turned_im = part_re * twist_im + part_im * twist_re
    final_re, final_im = phase_table(k_idx, k_idx, first_radix, 1.0)
    done_re, done_im = complex_product("rku,kv->rvu", turned_re, turned_im, final_re, final_im)
    return (done_re.reshape(row_count, length), done_im.reshape(row_count, length))


def wavenumbers(indices, length):
    signed = jnp.where(indices < length // 2, indices, indices - length)
    return (two_pi / length * signed.astype(jnp.float32), indices != length // 2)


def folded_spectra(spectrum, col_idx, ray_all):
    k_count, _, m_count, col_count = spectrum.shape
    length = k_count * m_count
    norm_factor = float(length * length)
    wave_col, retain_col = wavenumbers(col_idx, length)
    weight = jnp.where(col_idx == 0, 1.0, 2.0).astype(jnp.float32)
    row_idx = (
        jnp.arange(k_count, dtype=jnp.int32)[:, None]
        + k_count * jnp.arange(m_count, dtype=jnp.int32)[None, :]
    )
    wave_row, retain_row = wavenumbers(row_idx, length)
    wave_row = wave_row[:, None, :, None]
    retain_row = retain_row[:, None, :, None]
    squared = wave_col * wave_col + wave_row * wave_row
    retain = retain_row & retain_col & (squared > 0.0)
    safe_sq = jnp.where(retain, squared, 1.0)
    kernel = jnp.where(retain, -2.0 / (safe_sq * norm_factor), 0.0) * weight
    phi = kernel * spectrum
    terms = jnp.stack([phi, wave_row * phi, wave_row * wave_row * phi])
    terms = terms.reshape(3, k_count // ray_all, ray_all, 2, m_count, col_count)
    return jnp.transpose(jnp.sum(terms, axis=(1, 4)), (0, 2, 1, 3))


def per_device(density, lens_weight, plane_count, ray_state):
    sky_count = lax.axis_size("sky")
    sky_index = lax.axis_index("sky")
    ray_split = ray_state.shape[1] // 3
    ray_first = shifted(ray_state[:, :ray_split], "los", HOPS)
    ray_second = shifted(ray_state[:, ray_split:], "los", HOPS)
    plane_cells = density[0]
    length = plane_cells.shape[1]
    second = length // first_radix
    half = second // 2
    ray_dev = ray_state.shape[2]
    ray_all = ray_dev * sky_count
    strength = lens_weight[0] * plane_count[0].astype(jnp.float32)
    rows = rows_forward(plane_cells)
    ray_first, rows = lax.optimization_barrier((ray_first, rows))
    spread = lax.all_to_all(rows, "sky", split_axis=1, concat_axis=0, tiled=True)
    k_local = spread.shape[1]
    spread_re = spread[:, :, :half].reshape(length, k_local * half)
    spread_im = spread[:, :, half:].reshape(length, k_local * half)
    spectrum = columns_forward(spread_re, spread_im)
    ray_second, spectrum = lax.optimization_barrier((ray_second, spectrum))
    position = jnp.arange(k_local * half, dtype=jnp.int32)
    col_idx = sky_index * k_local + position // half + first_radix * (position % half)
    folds = folded_spectra(spectrum, col_idx, ray_all)
    q_idx = jnp.arange(ray_all, dtype=jnp.int32)
    back = block_table(q_idx, q_idx, ray_all, 1.0)
    at_rows = mixed("pjc,jn->pnc", folds.reshape(3, 2 * ray_all, k_local * half), back)
    at_rows = at_rows.reshape(3, 2, ray_all, k_local, half)
    returned = lax.all_to_all(at_rows, "sky", split_axis=2, concat_axis=3, tiled=True)
    k_all = returned.shape[3]
    dense = returned.reshape(3 * 2 * ray_dev, k_all * half) * strength
    arrived = jnp.stack(
        [shifted(dense, "los", HOPS - step_index) for step_index in range(HOPS)]
    ).reshape(HOPS, 3, 2, ray_dev, k_all, half)
    kx_idx = (
        jnp.arange(k_all, dtype=jnp.int32)[:, None]
        + first_radix * jnp.arange(half, dtype=jnp.int32)[None, :]
    )
    wave_col = wavenumbers(kx_idx, length)[0]
    f0_re, f0_im = (arrived[:, 0, 0], arrived[:, 0, 1])
    f1_re, f1_im = (arrived[:, 1, 0], arrived[:, 1, 1])
    f2_re, f2_im = (arrived[:, 2, 0], arrived[:, 2, 1])
    col_sq = wave_col * wave_col
    all_re = jnp.stack(
        [-wave_col * f0_im, -f1_im, -col_sq * f0_re, -f2_re, -wave_col * f1_re], axis=1
    )
    all_im = jnp.stack(
        [wave_col * f0_re, f1_re, -col_sq * f0_im, -f2_im, -wave_col * f1_im], axis=1
    )
    flat_re = all_re.reshape(HOPS * 5 * ray_dev, k_all * half)
    flat_im = all_im.reshape(HOPS * 5 * ray_dev, k_all * half)
    field_re, _ = rows_inverse(flat_re, flat_im, length, half)
    fields = field_re.reshape(HOPS, 5, ray_dev, length)
    ray_tile = jnp.concatenate([ray_first, ray_second], axis=1)
    for step_index in range(HOPS):
        ray_tile = lens_step(ray_tile, fields[step_index][None])
    return ray_tile


def solution(mesh):
    return jax.shard_map(
        per_device,
        mesh=mesh,
        in_specs=(
            P(("real", "los"), "sky", None),
            P(("real", "los")),
            P(("real", "los")),
            P(("real", "los"), None, "sky", None),
        ),
        out_specs=P(("real", "los"), None, "sky", None),
        check_vma=False,
    )
```

profile of v0, /device:TPU:0, one launch (start us, length us, event | category | flops | bytes accessed | tf_op | source)
XLA Modules:
  0.0 212.5 jit_solution(7195133602715866516)
XLA Ops:
  0.0 1.9 slice.160
  1.9 4.0 %collective-permute-start = (f32[1,4,16,2048]{3,2,1,0:T(8,128)}, f32[1,4,16,2048]{3,2,1,0:T(8,128)S(1)}, u32[]{:S(2)}, u32[]{:S(2)}) collective-permute-start(f32[1,4,16,2048]{3,2,1,0:T(8,128)} %slice.160), channel_id=1, source_target_pairs={{8,0},{10,2},{12,4},{14,6},{0,8},{2,10},{4,12},{6,14},{9,1},{11,3}... | collective-permute-start | bytes 1572872 | tf_op jit(solution)/shard_map/ppermute | solution.py:16
  5.9 2.3 %slice.163 = f32[1,8,16,2048]{3,2,1,0:T(8,128)} slice(f32[1,12,16,2048]{3,2,1,0:T(8,128)} %param.7), slice={[0:1], [4:12], [0:16], [0:2048]} | slice | bytes 2097152 | tf_op jit(solution)/shard_map/slice | solution.py:197
  9.7 5.4 %copy.96 = f32[128,8,16,128]{3,2,1,0:T(8,128)S(1)} copy(f32[128,8,16,128]{3,1,2,0:T(8,128)} %bitcast.162) | data formatting | bytes 16777216
  15.0 6.0 %fusion.143 = f32[16,1024,128]{2,0,1:T(8,128)} fusion(f32[1024,16,128]{2,1,0:T(8,128)S(1)} %bitcast.149), kind=kOutput, calls=%fused_computation.239 | convolution fusion | flops 201330176 | bytes 16777216 | tf_op jit(solution)/shard_map/rvu,vk->rku/dot_general | solution.py:84
  22.4 10.8 %subtract_bitcast_fusion = (f32[1024,16,128]{2,1,0:T(8,128)}, f32[1024,16,128]{2,1,0:T(8,128)}) fusion(f32[16,1024,128]{2,0,1:T(8,128)} %fusion.143, f32[16,128]{1,0:T(8,128)S(1)} %get-tuple-element.89, f32[16,128]{1,0:T(8,128)S(1)} %get-tuple-element.90, f32[1024,16,128]{2,1,0:T(8,128)S(1)} %bitcast.150), kind=kOutput, calls=%fused_computation.9 | convolution fusion | flops 213913088 | bytes 33570816 | tf_op jit(solution)/shard_map/rvu,vk->rku/dot_general | solution.py:84
  33.2 9.6 %fusion.2 = f32[1024,16,128]{2,0,1:T(8,128)S(1)} fusion(f32[1024,16,128]{2,1,0:T(8,128)} %get-tuple-element.58, f32[128,64]{1,0:T(8,128)S(1)} %get-tuple-element.92, f32[128,64]{1,0:T(8,128)S(1)} %fusion.113), kind=kOutput, calls=%fused_computation.4 | convolution fusion | flops 1610629120 | bytes 16842752 | tf_op jit(solution)/shard_map/rkj,jn->rkn/dot_general | solution.py:84
  42.9 5.6 %fusion.15 = f32[1024,16,128]{2,0,1:T(8,128)S(1)} fusion(f32[1024,16,128]{2,0,1:T(8,128)S(1)} %fusion.2, f32[1024,16,128]{2,1,0:T(8,128)S(1)} %bitcast.155, f32[128,64]{1,0:T(8,128)S(1)} %get-tuple-element.91, f32[128,64]{1,0:T(8,128)S(1)} %get-tuple-element.92), kind=kOutput, calls=%fused_computation.26 | convolution fusion | flops 1612726272 | bytes 25231360 | tf_op jit(solution)/shard_map/rkj,jn->rkn/dot_general | solution.py:84
  48.4 3.6 %fusion.9 = f32[64,32,512]{2,1,0:T(8,128)} fusion(f32[512]{0:T(512)S(1)} %get-tuple-element.100, f32[64,32]{1,0:T(8,128)S(1)} %get-tuple-element.87, f32[512]{0:T(512)S(1)} %get-tuple-element.99, pred[512]{0:T(512)(128)(4,1)S(1)} %broadcast_compare_fusion, pred[64,32]{1,0:T(8,128)(4,1)S(1)} %fusion.108), kind=kLoop, calls=%fused_computation.15 | loop fusion | flops 9437184 | bytes 4209152 | tf_op jit(solution)/shard_map/mul | solution.py:185
  52.0 0.6 collective-permute-done
  52.6 10.9 %all_to_all.27 = f32[1024,16,128]{2,0,1:T(8,128)S(1)} all-to-all(f32[1024,16,128]{2,0,1:T(8,128)S(1)} %fusion.15), channel_id=1, replica_groups=mesh['real'=2,'los'=8,'sky'=2] {'sky'}, dimensions={1} | all-to-all | bytes 16777216 | tf_op jit(solution)/shard_map/all_to_all | solution.py:207
  63.5 4.9 %copy.76 = f32[1024,2,8,128]{3,2,0,1:T(8,128)S(1)} copy(f32[1024,2,8,128]{3,0,2,1:T(8,128)S(1)} %bitcast.157) | data formatting | bytes 16777216 | tf_op jit(solution)/shard_map/all_to_all | solution.py:207
  68.4 7.2 %fusion.237 = (f32[2048,8,64]{2,1,0:T(8,128)}, f32[2048,8,64]{2,1,0:T(8,128)}) fusion(f32[2048,8,128]{2,1,0:T(8,128)S(1)} %bitcast.148), kind=kLoop, calls=%fused_computation.331 | loop fusion | bytes 16777216 | tf_op jit(solution)/shard_map/slice | solution.py:209
  75.5 7.5 %reshape_reshape.14 = f32[64,32,512]{2,1,0:T(8,128)} reshape(f32[2048,8,64]{2,1,0:T(8,128)} %get-tuple-element.62) | data formatting | bytes 8388608 | tf_op jit(solution)/shard_map/reshape;reshape | solution.py:133
  83.0 7.5 %reshape_reshape.13 = f32[64,32,512]{2,1,0:T(8,128)} reshape(f32[2048,8,64]{2,1,0:T(8,128)} %get-tuple-element.61) | data formatting | bytes 8388608 | tf_op jit(solution)/shard_map/reshape;reshape | solution.py:132
  90.5 9.4 %fusion.10 = f32[128,32,512]{2,0,1:T(8,128)S(1)} fusion(f32[64,32,512]{2,1,0:T(8,128)} %reshape_reshape.14, f32[64,64]{1,0:T(8,128)S(1)} %get-tuple-element.93, f32[64,64]{1,0:T(8,128)S(1)} %get-tuple-element.94), kind=kOutput, calls=%fused_computation.16 | convolution fusion | flops 805314560 | bytes 12615680 | tf_op jit(solution)/shard_map/jn,jbc->nbc/dot_general | solution.py:84
  100.0 5.9 %fusion.18 = f32[128,32,512]{2,0,1:T(8,128)S(1)} fusion(f32[128,32,512]{2,0,1:T(8,128)S(1)} %fusion.10, f32[64,32,512]{2,1,0:T(8,128)S(1)} %copy-done, f32[64,64]{1,0:T(8,128)S(1)} %fusion.127, f32[64,64]{1,0:T(8,128)S(1)} %get-tuple-element.93), kind=kOutput, calls=%fused_computation.27 | convolution fusion | flops 807411712 | bytes 21004288 | tf_op jit(solution)/shard_map/jn,jbc->nbc/dot_general | solution.py:84
  105.9 1.1 subtract_bitcast_fusion.1
  107.1 1.8 pad_maximum_fusion
  108.9 8.7 %fusion = f32[64,64,512]{2,0,1:T(8,128)S(1)} fusion(f32[64,64,512]{2,0,1:T(8,128)S(1)} %bitcast.152, f32[32,32]{0,1:T(8,128)S(1)} %get-tuple-element.98, f32[32,32]{0,1:T(8,128)S(1)} %fusion.164, f32[32,32]{0,1:T(8,128)S(1)} %get-tuple-element.97), kind=kOutput, calls=%fused_computation.2 | convolution fusion | flops 805318656 | bytes 16789504 | tf_op jit(solution)/shard_map/kjc,jn->knc/dot_general | solution.py:84
  117.6 4.0 %broadcast_multiply_fusion.1 = (f32[64,2,32,512]{3,2,1,0:T(8,128)}, f32[64,2,32,512]{3,2,1,0:T(8,128)S(1)}) fusion(f32[64,32]{1,0:T(8,128)S(1)} %get-tuple-element.88, f32[64,2,32,512]{3,2,1,0:T(8,128)S(1)} %bitcast.153, f32[64,32,512]{2,1,0:T(8,128)S(1)} %copy-done.1), kind=kLoop, calls=%fused_computation.21 | loop fusion | flops 4194304 | bytes 29368320 | tf_op jit(solution)/shard_map/mul | solution.py:187
  121.6 0.6 broadcast_multiply_fusion
  122.3 7.4 %maximum_reduce_fusion = f32[3,32,2,512]{3,2,1,0:T(2,128)S(1)} fusion(f32[1,2,32,2,32,512]{5,4,3,2,1,0:T(8,128)S(1)} %bitcast.151, f32[1,2,32,2,32,512]{5,4,3,2,1,0:T(8,128)} %bitcast.156, f32[1,2,32,2,32,512]{5,4,3,2,1,0:T(8,128)S(1)} %bitcast.147), kind=kLoop, calls=%fused_computation | loop fusion | flops 18776064 | bytes 25559040 | tf_op jit(solution)/shard_map/reduce_sum | solution.py:189
  129.7 0.4 convolution_bitcast_fusion
  130.3 0.5 reshape.942
  130.8 4.0 %all_to_all.28 = f32[2,1,49152]{2,1,0:T(1,128)S(1)} all-to-all(f32[2,1,49152]{2,1,0:T(1,128)S(1)} %reshape.942), channel_id=1, replica_groups=mesh['real'=2,'los'=8,'sky'=2] {'sky'}, dimensions={0} | all-to-all | bytes 786432 | tf_op jit(solution)/shard_map/all_to_all | solution.py:220
  134.9 0.6 broadcast.706
  135.4 1.9 reduce
  137.3 0.5 reshape.943
  138.2 2.4 %collective-permute-start.2 = (f32[96,1024]{1,0:T(8,128)S(1)}, f32[96,1024]{1,0:T(8,128)S(1)}, u32[]{:S(2)}, u32[]{:S(2)}) collective-permute-start(f32[96,1024]{1,0:T(8,128)S(1)} %mul.1433), channel_id=1, source_target_pairs={{8,0},{10,2},{12,4},{14,6},{0,8},{2,10},{4,12},{6,14},{9,1},{11,3}... | collective-permute-start | bytes 1179656 | tf_op jit(solution)/shard_map/ppermute | solution.py:16
  140.6 2.5 %collective-permute-start.3 = (f32[96,1024]{1,0:T(8,128)S(1)}, f32[96,1024]{1,0:T(8,128)S(1)}, u32[]{:S(2)}, u32[]{:S(2)}) collective-permute-start(f32[96,1024]{1,0:T(8,128)S(1)} %mul.1433), channel_id=1, source_target_pairs={{10,0},{12,2},{14,4},{0,6},{2,8},{4,10},{6,12},{8,14},{11,1},{13,3... | collective-permute-start | bytes 1179656 | tf_op jit(solution)/shard_map/ppermute | solution.py:16
  143.1 1.0 collective-permute-start.5
  144.1 0.6 multiply_sine_fusion.2
  144.8 0.6 fusion.140
  145.4 30.2 %collective-permute-done.2 = f32[96,1024]{1,0:T(8,128)S(1)} collective-permute-done((f32[96,1024]{1,0:T(8,128)S(1)}, f32[96,1024]{1,0:T(8,128)S(1)}, u32[]{:S(2)}, u32[]{:S(2)}) %collective-permute-start.2) | collective-permute-done | bytes 393248 | tf_op jit(solution)/shard_map/ppermute | solution.py:16
  175.8 17.9 %collective-permute-done.3 = f32[96,1024]{1,0:T(8,128)S(1)} collective-permute-done((f32[96,1024]{1,0:T(8,128)S(1)}, f32[96,1024]{1,0:T(8,128)S(1)}, u32[]{:S(2)}, u32[]{:S(2)}) %collective-permute-start.3) | collective-permute-done | bytes 393248 | tf_op jit(solution)/shard_map/ppermute | solution.py:16
  194.7 0.4 copy-done.11
  195.7 1.3 fusion.102
  197.0 1.3 fusion.98
  198.3 1.3 convolution_subtract_fusion
  199.7 1.4 convolution_add_fusion
  201.1 1.3 fusion.21
  202.4 1.3 subtract_bitcast_fusion.2
  204.3 2.2 %add_subtract_fusion.6 = (f32[1,1,16,2048]{3,2,1,0:T(8,128)S(1)}, f32[1,1,16,2048]{3,2,1,0:T(8,128)S(1)}, f32[1,1,16,2048]{3,2,1,0:T(8,128)S(1)}, f32[1,1,16,204...) fusion(f32[1,5,16,2048]{3,2,1,0:T(8,128)S(1)} %slice.181, f32[1,8,16,2048]{3,2,1,0:T(8,128)} %copy-done.2, ...), kind=kLoop, calls=%fused_computation.99 | loop fusion | flops 917504 | bytes 2490368 | tf_op jit(solution)/shard_map/sub | solution.py:44
  206.5 1.9 fusion.55
  208.6 1.2 fusion.51
  210.4 1.1 copy-done.12
  211.6 0.7 constant_dynamic-update-slice_fusion
  (83 shorter events, 4.9 us)
Async XLA Ops:
  1.9 50.7 %collective-permute-start = (f32[1,4,16,2048]{3,2,1,0:T(8,128)}, f32[1,4,16,2048]{3,2,1,0:T(8,128)S(1)}, u32[]{:S(2)}, u32[]{:S(2)}) collective-permute-start(f32[1,4,16,2048]{3,2,1,0:T(8,128)} %slice.160), channel_id=1, source_target_pairs={{8,0},{10,2},{12,4},{14,6},{0,8},{2,10},{4,12},{6,14},{9,1},{11,3}... | collective-permute-start | bytes 1572872 | tf_op jit(solution)/shard_map/ppermute | solution.py:16
  8.2 109.4 %collective-permute-start.1 = (f32[1,8,16,2048]{3,2,1,0:T(8,128)}, f32[1,8,16,2048]{3,2,1,0:T(8,128)S(1)}, u32[]{:S(2)}, u32[]{:S(2)}) collective-permute-start(f32[1,8,16,2048]{3,2,1,0:T(8,128)} %slice.163), channel_id=1, source_target_pairs={{8,0},{10,2},{12,4},{14,6},{0,8},{2,10},{4,12},{6,14},{9,1},{11,3}... | collective-permute-start | bytes 3145736 | tf_op jit(solution)/shard_map/ppermute | solution.py:16
  33.2 9.6 %slice-start = ((s8[8388608]{0:T(1024)(128)(4,1)}), s8[4194304]{0:T(1024)(128)(4,1)S(1)}, s32[]{:S(2)}) async-start(s8[8388608]{0:T(1024)(128)(4,1)} %bitcast.154), calls=%async_computation.2 | async-start | bytes 8388608
  33.2 9.6 %slice-start.1 = ((s8[8388608]{0:T(1024)(128)(4,1)}), s8[4194304]{0:T(1024)(128)(4,1)S(1)}, s32[]{:S(2)}) async-start(s8[8388608]{0:T(1024)(128)(4,1)} %bitcast.154), calls=%async_computation.3 | async-start | bytes 8388608
  52.6 10.9 %copy-start.4 = (f32[1,4,16,2048]{3,2,1,0:T(8,128)}, f32[1,4,16,2048]{3,2,1,0:T(8,128)S(1)}, u32[]{:S(2)}) copy-start(f32[1,4,16,2048]{3,2,1,0:T(8,128)S(1)} %collective-permute-done) | copy-start | bytes 1572868
  90.5 9.4 %copy-start = (f32[64,32,512]{2,1,0:T(8,128)S(1)}, f32[64,32,512]{2,1,0:T(8,128)}, u32[]{:S(2)}) copy-start(f32[64,32,512]{2,1,0:T(8,128)} %reshape_reshape.13) | copy-start | bytes 12582916
  108.9 8.8 %copy-start.1 = (f32[64,32,512]{2,1,0:T(8,128)S(1)}, f32[64,32,512]{2,1,0:T(8,128)}, u32[]{:S(2)}) copy-start(f32[64,32,512]{2,1,0:T(8,128)} %fusion.9) | copy-start | bytes 12582916
  117.6 4.0 %copy-start.2 = (f32[1,8,16,2048]{3,2,1,0:T(8,128)}, f32[1,8,16,2048]{3,2,1,0:T(8,128)S(1)}, u32[]{:S(2)}) copy-start(f32[1,8,16,2048]{3,2,1,0:T(8,128)S(1)} %collective-permute-done.1) | copy-start | bytes 3145732
  138.2 37.4 %collective-permute-start.2 = (f32[96,1024]{1,0:T(8,128)S(1)}, f32[96,1024]{1,0:T(8,128)S(1)}, u32[]{:S(2)}, u32[]{:S(2)}) collective-permute-start(f32[96,1024]{1,0:T(8,128)S(1)} %mul.1433), channel_id=1, source_target_pairs={{8,0},{10,2},{12,4},{14,6},{0,8},{2,10},{4,12},{6,14},{9,1},{11,3}... | collective-permute-start | bytes 1179656 | tf_op jit(solution)/shard_map/ppermute | solution.py:16
  140.6 53.2 %collective-permute-start.3 = (f32[96,1024]{1,0:T(8,128)S(1)}, f32[96,1024]{1,0:T(8,128)S(1)}, u32[]{:S(2)}, u32[]{:S(2)}) collective-permute-start(f32[96,1024]{1,0:T(8,128)S(1)} %mul.1433), channel_id=1, source_target_pairs={{10,0},{12,2},{14,4},{0,6},{2,8},{4,10},{6,12},{8,14},{11,1},{13,3... | collective-permute-start | bytes 1179656 | tf_op jit(solution)/shard_map/ppermute | solution.py:16
  143.1 50.8 %collective-permute-start.4 = (f32[96,1024]{1,0:T(8,128)S(1)}, f32[96,1024]{1,0:T(8,128)S(1)}, u32[]{:S(2)}, u32[]{:S(2)}) collective-permute-start(f32[96,1024]{1,0:T(8,128)S(1)} %mul.1433), channel_id=1, source_target_pairs={{12,0},{14,2},{0,4},{2,6},{4,8},{6,10},{8,12},{10,14},{13,1},{15,3... | collective-permute-start | bytes 1179656 | tf_op jit(solution)/shard_map/ppermute | solution.py:16
  143.1 51.1 %collective-permute-start.5 = (f32[96,1024]{1,0:T(8,128)S(1)}, f32[96,1024]{1,0:T(8,128)S(1)}, u32[]{:S(2)}, u32[]{:S(2)}) collective-permute-start(f32[96,1024]{1,0:T(8,128)S(1)} %mul.1433), channel_id=1, source_target_pairs={{14,0},{0,2},{2,4},{4,6},{6,8},{8,10},{10,12},{12,14},{15,1},{1,3}... | collective-permute-start | bytes 1179656 | tf_op jit(solution)/shard_map/ppermute | solution.py:16
  194.4 0.7 copy-start.11
  194.7 0.7 copy-start.10
  199.7 1.4 copy-start.9
  204.3 4.3 %copy-start.5 = (f32[1,4,16,2048]{3,2,1,0:T(8,128)S(1)}, f32[1,4,16,2048]{3,2,1,0:T(8,128)}, u32[]{:S(2)}) copy-start(f32[1,4,16,2048]{3,2,1,0:T(8,128)} %copy-done.4) | copy-start | bytes 1572868
  208.5 1.4 copy-start.3
  208.5 1.4 copy-start.6
  208.5 1.4 copy-start.7
  208.5 1.5 copy-start.8
  210.4 1.1 copy-start.12
where the time goes:
time: 217 us; the launch traced here: 212 us
  matrix products  64.5 us (30%)
  waiting for transfers between devices  48.7 us (22%)
  local copies, waits for them, and re-layouts  42.6 us (20%)
  other arithmetic  29.5 us (14%)
  blocking collectives  15 us (7%)
  starting transfers between devices  10 us (5%)
  between operations  2.2 us (1%)
    dot_general x14, matrix products, mixed(): jnp.einsum(form, left_op, right_op, precision=highest, preferred_element_...  64.5 us
    ppermute x6, waiting for transfers between devices, shifted(): return lax.ppermute(block, axis, route)  48.7 us
    all_to_all x1, blocking collectives, per_device(): lax.all_to_all(rows, 'sky', split_axis=1, concat_axis=0, tiled=True)  10.9 us
    ppermute x6, starting transfers between devices, shifted(): return lax.ppermute(block, axis, route)  10 us
    unnamed x38, local copies, waits for them, and re-layouts  8.15 us
    another operation x1, local copies, waits for them, and re-layouts, columns_forward(): spread_im.reshape(factor_one, second, col_count)  7.53 us
    another operation x1, local copies, waits for them, and re-layouts, columns_forward(): spread_re.reshape(factor_one, second, col_count)  7.51 us
    reduce_sum x1, other arithmetic, folded_spectra(): return jnp.transpose(jnp.sum(terms, axis=(1, 4)), (0, 2, 1, 3))  7.37 us
  transfers between devices with their start and end apart: 6, of which 3 were waited for; matrix products, arithmetic and copies ran while one was open for 47% of the time, Pallas kernels for 0%

commit v1 on v0

--- a/solution.py
+++ b/solution.py
@@ -8,6 +8,12 @@
 two_pi = 2.0 * math.pi
 highest = lax.Precision.HIGH
 first_radix = 16
+
+
+def exchange_blocks(x, name, split, join):
+    pieces = jnp.split(x, lax.axis_size(name), axis=split)
+    arrived = lax.all_to_all(jnp.stack(pieces), name, 0, 0)
+    return jnp.concatenate(arrived, axis=join)
 
 
 def shifted(block, axis, distance):
@@ -204,7 +210,7 @@
     strength = lens_weight[0] * plane_count[0].astype(jnp.float32)
     rows = rows_forward(plane_cells)
     ray_first, rows = lax.optimization_barrier((ray_first, rows))
-    spread = lax.all_to_all(rows, "sky", split_axis=1, concat_axis=0, tiled=True)
+    spread = exchange_blocks(rows, "sky", 1, 0)
     k_local = spread.shape[1]
     spread_re = spread[:, :, :half].reshape(length, k_local * half)
     spread_im = spread[:, :, half:].reshape(length, k_local * half)

time: 217 us -> 218 us (level)
  transfers between devices with their start and end apart: 6 -> 6, of which waited for: 3 -> 3; matrix products, arithmetic and copies ran while one was open for 47% -> 48% of each run, Pallas kernels for 0% -> 0%
where the time goes in v1:
time: 218 us; the launch traced here: 214 us
  matrix products  64.5 us (30%)
  waiting for transfers between devices  48.8 us (22%)
  local copies, waits for them, and re-layouts  43.3 us (20%)
  other arithmetic  30 us (14%)
  blocking collectives  15 us (7%)
  starting transfers between devices  9.98 us (5%)
  between operations  2.21 us (1%)
    dot_general x14, matrix products, mixed(): jnp.einsum(form, left_op, right_op, precision=highest, preferred_element_...  64.5 us
    ppermute x6, waiting for transfers between devices, shifted(): return lax.ppermute(block, axis, route)  48.8 us
    all_to_all x1, blocking collectives, exchange_blocks(): arrived = lax.all_to_all(jnp.stack(pieces), name, 0, 0)  10.9 us
    ppermute x6, starting transfers between devices, shifted(): return lax.ppermute(block, axis, route)  9.98 us
    unnamed x38, local copies, waits for them, and re-layouts  8.19 us
    another operation x1, local copies, waits for them, and re-layouts, columns_forward(): spread_re.reshape(factor_one, second, col_count)  7.52 us
    another operation x1, local copies, waits for them, and re-layouts, columns_forward(): spread_im.reshape(factor_one, second, col_count)  7.51 us
    reduce_sum x1, other arithmetic, folded_spectra(): return jnp.transpose(jnp.sum(terms, axis=(1, 4)), (0, 2, 1, 3))  7.37 us
  transfers between devices with their start and end apart: 6, of which 3 were waited for; matrix products, arithmetic and copies ran while one was open for 48% of the time, Pallas kernels for 0%

profile of v1, /device:TPU:0, one launch (start us, length us, event | category | flops | bytes accessed | tf_op | source)
XLA Modules:
  0.0 213.7 jit_solution(11504497219756428325)
XLA Ops:
  0.0 1.9 slice.160
  1.9 4.0 %collective-permute-start = (f32[1,4,16,2048]{3,2,1,0:T(8,128)}, f32[1,4,16,2048]{3,2,1,0:T(8,128)S(1)}, u32[]{:S(2)}, u32[]{:S(2)}) collective-permute-start(f32[1,4,16,2048]{3,2,1,0:T(8,128)} %slice.160), channel_id=1, source_target_pairs={{8,0},{10,2},{12,4},{14,6},{0,8},{2,10},{4,12},{6,14},{9,1},{11,3}... | collective-permute-start | bytes 1572872 | tf_op jit(solution)/shard_map/ppermute | solution.py:22
  5.9 2.3 %slice.163 = f32[1,8,16,2048]{3,2,1,0:T(8,128)} slice(f32[1,12,16,2048]{3,2,1,0:T(8,128)} %param.7), slice={[0:1], [4:12], [0:16], [0:2048]} | slice | bytes 2097152 | tf_op jit(solution)/shard_map/slice | solution.py:203
  9.7 5.4 %copy.96 = f32[128,8,16,128]{3,2,1,0:T(8,128)S(1)} copy(f32[128,8,16,128]{3,1,2,0:T(8,128)} %bitcast.162) | data formatting | bytes 16777216
  15.0 6.0 %fusion.143 = f32[16,1024,128]{2,0,1:T(8,128)} fusion(f32[1024,16,128]{2,1,0:T(8,128)S(1)} %bitcast.150), kind=kOutput, calls=%fused_computation.242 | convolution fusion | flops 201330176 | bytes 16777216 | tf_op jit(solution)/shard_map/rvu,vk->rku/dot_general | solution.py:90
  22.4 10.8 %subtract_bitcast_fusion = (f32[1024,16,128]{2,1,0:T(8,128)}, f32[1024,16,128]{2,1,0:T(8,128)}) fusion(f32[16,1024,128]{2,0,1:T(8,128)} %fusion.143, f32[16,128]{1,0:T(8,128)S(1)} %get-tuple-element.91, f32[16,128]{1,0:T(8,128)S(1)} %get-tuple-element.92, f32[1024,16,128]{2,1,0:T(8,128)S(1)} %bitcast.151), kind=kOutput, calls=%fused_computation.10 | convolution fusion | flops 213913088 | bytes 33570816 | tf_op jit(solution)/shard_map/rvu,vk->rku/dot_general | solution.py:90
  33.2 9.6 %fusion.2 = f32[1024,16,128]{2,0,1:T(8,128)S(1)} fusion(f32[1024,16,128]{2,1,0:T(8,128)} %get-tuple-element.58, f32[128,64]{1,0:T(8,128)S(1)} %get-tuple-element.94, f32[128,64]{1,0:T(8,128)S(1)} %fusion.113), kind=kOutput, calls=%fused_computation.5 | convolution fusion | flops 1610629120 | bytes 16842752 | tf_op jit(solution)/shard_map/rkj,jn->rkn/dot_general | solution.py:90
  42.8 5.6 %fusion.15 = f32[1024,16,128]{2,0,1:T(8,128)S(1)} fusion(f32[1024,16,128]{2,0,1:T(8,128)S(1)} %fusion.2, f32[1024,16,128]{2,1,0:T(8,128)S(1)} %bitcast.156, f32[128,64]{1,0:T(8,128)S(1)} %get-tuple-element.93, f32[128,64]{1,0:T(8,128)S(1)} %get-tuple-element.94), kind=kOutput, calls=%fused_computation.29 | convolution fusion | flops 1612726272 | bytes 25231360 | tf_op jit(solution)/shard_map/rkj,jn->rkn/dot_general | solution.py:90
  48.4 3.6 %fusion.9 = f32[64,32,512]{2,1,0:T(8,128)} fusion(f32[512]{0:T(512)S(1)} %get-tuple-element.102, f32[64,32]{1,0:T(8,128)S(1)} %get-tuple-element.89, f32[512]{0:T(512)S(1)} %get-tuple-element.101, pred[512]{0:T(512)(128)(4,1)S(1)} %broadcast_compare_fusion, pred[64,32]{1,0:T(8,128)(4,1)S(1)} %fusion.108), kind=kLoop, calls=%fused_computation.16 | loop fusion | flops 9437184 | bytes 4209152 | tf_op jit(solution)/shard_map/mul | solution.py:191
  52.0 0.6 collective-permute-done
  52.6 0.8 slice_bitcast_fusion.1
  53.4 0.6 pad_maximum_fusion
  54.0 10.9 %all_to_all.14 = f32[2,1024,8,128]{3,1,2,0:T(8,128)S(1)} all-to-all(f32[2,1024,8,128]{3,1,2,0:T(8,128)S(1)} %pad_maximum_fusion), channel_id=1, replica_groups=mesh['real'=2,'los'=8,'sky'=2] {'sky'}, dimensions={0} | all-to-all | bytes 16777216 | tf_op jit(solution)/shard_map/all_to_all | solution.py:15
  64.9 4.9 %copy.76 = f32[2,1024,8,128]{3,2,1,0:T(8,128)S(1)} copy(f32[2,1024,8,128]{3,1,2,0:T(8,128)S(1)} %all_to_all.14) | data formatting | bytes 16777216 | tf_op jit(solution)/shard_map/all_to_all | solution.py:15
  69.8 7.1 %fusion.237 = (f32[2048,8,64]{2,1,0:T(8,128)}, f32[2048,8,64]{2,1,0:T(8,128)}) fusion(f32[2048,8,128]{2,1,0:T(8,128)S(1)} %bitcast.149), kind=kLoop, calls=%fused_computation.334 | loop fusion | bytes 16777216 | tf_op jit(solution)/shard_map/slice | solution.py:215
  76.9 7.5 %reshape_reshape.14 = f32[64,32,512]{2,1,0:T(8,128)} reshape(f32[2048,8,64]{2,1,0:T(8,128)} %get-tuple-element.62) | data formatting | bytes 8388608 | tf_op jit(solution)/shard_map/reshape;reshape | solution.py:139
  84.4 7.5 %reshape_reshape.13 = f32[64,32,512]{2,1,0:T(8,128)} reshape(f32[2048,8,64]{2,1,0:T(8,128)} %get-tuple-element.61) | data formatting | bytes 8388608 | tf_op jit(solution)/shard_map/reshape;reshape | solution.py:138
  91.9 9.4 %fusion.10 = f32[128,32,512]{2,0,1:T(8,128)S(1)} fusion(f32[64,32,512]{2,1,0:T(8,128)} %reshape_reshape.14, f32[64,64]{1,0:T(8,128)S(1)} %get-tuple-element.95, f32[64,64]{1,0:T(8,128)S(1)} %get-tuple-element.96), kind=kOutput, calls=%fused_computation.17 | convolution fusion | flops 805314560 | bytes 12615680 | tf_op jit(solution)/shard_map/jn,jbc->nbc/dot_general | solution.py:90
  101.4 5.9 %fusion.18 = f32[128,32,512]{2,0,1:T(8,128)S(1)} fusion(f32[128,32,512]{2,0,1:T(8,128)S(1)} %fusion.10, f32[64,32,512]{2,1,0:T(8,128)S(1)} %copy-done, f32[64,64]{1,0:T(8,128)S(1)} %fusion.127, f32[64,64]{1,0:T(8,128)S(1)} %get-tuple-element.95), kind=kOutput, calls=%fused_computation.30 | convolution fusion | flops 807411712 | bytes 21004288 | tf_op jit(solution)/shard_map/jn,jbc->nbc/dot_general | solution.py:90
  107.3 1.1 subtract_bitcast_fusion.1
  108.4 1.8 pad_maximum_fusion.1
  110.3 8.7 %fusion = f32[64,64,512]{2,0,1:T(8,128)S(1)} fusion(f32[64,64,512]{2,0,1:T(8,128)S(1)} %bitcast.153, f32[32,32]{0,1:T(8,128)S(1)} %get-tuple-element.100, f32[32,32]{0,1:T(8,128)S(1)} %fusion.164, f32[32,32]{0,1:T(8,128)S(1)} %get-tuple-element.99), kind=kOutput, calls=%fused_computation.3 | convolution fusion | flops 805318656 | bytes 16789504 | tf_op jit(solution)/shard_map/kjc,jn->knc/dot_general | solution.py:90
  119.0 4.0 %broadcast_multiply_fusion.1 = (f32[64,2,32,512]{3,2,1,0:T(8,128)}, f32[64,2,32,512]{3,2,1,0:T(8,128)S(1)}) fusion(f32[64,32]{1,0:T(8,128)S(1)} %get-tuple-element.90, f32[64,2,32,512]{3,2,1,0:T(8,128)S(1)} %bitcast.154, f32[64,32,512]{2,1,0:T(8,128)S(1)} %copy-done.1), kind=kLoop, calls=%fused_computation.22 | loop fusion | flops 4194304 | bytes 29368320 | tf_op jit(solution)/shard_map/mul | solution.py:193
  123.0 0.6 broadcast_multiply_fusion
  123.7 7.4 %maximum_reduce_fusion = f32[3,32,2,512]{3,2,1,0:T(2,128)S(1)} fusion(f32[1,2,32,2,32,512]{5,4,3,2,1,0:T(8,128)S(1)} %bitcast.152, f32[1,2,32,2,32,512]{5,4,3,2,1,0:T(8,128)} %bitcast.157, f32[1,2,32,2,32,512]{5,4,3,2,1,0:T(8,128)S(1)} %bitcast.148), kind=kLoop, calls=%fused_computation | loop fusion | flops 18776064 | bytes 25559040 | tf_op jit(solution)/shard_map/reduce_sum | solution.py:195
  131.7 0.5 reshape.946
  132.2 4.0 %all_to_all.15 = f32[2,1,49152]{2,1,0:T(1,128)S(1)} all-to-all(f32[2,1,49152]{2,1,0:T(1,128)S(1)} %reshape.946), channel_id=1, replica_groups=mesh['real'=2,'los'=8,'sky'=2] {'sky'}, dimensions={0} | all-to-all | bytes 786432 | tf_op jit(solution)/shard_map/all_to_all | solution.py:226
  136.3 0.5 broadcast.706
  136.7 1.8 reduce
  138.5 0.5 reshape.947
  139.4 2.4 %collective-permute-start.2 = (f32[96,1024]{1,0:T(8,128)S(1)}, f32[96,1024]{1,0:T(8,128)S(1)}, u32[]{:S(2)}, u32[]{:S(2)}) collective-permute-start(f32[96,1024]{1,0:T(8,128)S(1)} %mul.1433), channel_id=1, source_target_pairs={{8,0},{10,2},{12,4},{14,6},{0,8},{2,10},{4,12},{6,14},{9,1},{11,3}... | collective-permute-start | bytes 1179656 | tf_op jit(solution)/shard_map/ppermute | solution.py:22
  141.8 2.5 %collective-permute-start.3 = (f32[96,1024]{1,0:T(8,128)S(1)}, f32[96,1024]{1,0:T(8,128)S(1)}, u32[]{:S(2)}, u32[]{:S(2)}) collective-permute-start(f32[96,1024]{1,0:T(8,128)S(1)} %mul.1433), channel_id=1, source_target_pairs={{10,0},{12,2},{14,4},{0,6},{2,8},{4,10},{6,12},{8,14},{11,1},{13,3... | collective-permute-start | bytes 1179656 | tf_op jit(solution)/shard_map/ppermute | solution.py:22
  144.3 1.0 collective-permute-start.5
  145.3 0.7 multiply_sine_fusion.2
  146.0 0.6 fusion.140
  146.6 30.2 %collective-permute-done.2 = f32[96,1024]{1,0:T(8,128)S(1)} collective-permute-done((f32[96,1024]{1,0:T(8,128)S(1)}, f32[96,1024]{1,0:T(8,128)S(1)}, u32[]{:S(2)}, u32[]{:S(2)}) %collective-permute-start.2) | collective-permute-done | bytes 393248 | tf_op jit(solution)/shard_map/ppermute | solution.py:22
  177.0 17.9 %collective-permute-done.3 = f32[96,1024]{1,0:T(8,128)S(1)} collective-permute-done((f32[96,1024]{1,0:T(8,128)S(1)}, f32[96,1024]{1,0:T(8,128)S(1)}, u32[]{:S(2)}, u32[]{:S(2)}) %collective-permute-start.3) | collective-permute-done | bytes 393248 | tf_op jit(solution)/shard_map/ppermute | solution.py:22
  196.9 1.3 fusion.102
  198.2 1.3 fusion.98
  199.5 1.3 convolution_subtract_fusion
  200.9 1.4 convolution_add_fusion
  202.3 1.3 fusion.21
  203.6 1.3 subtract_bitcast_fusion.2
  205.5 2.2 %add_subtract_fusion.6 = (f32[1,1,16,2048]{3,2,1,0:T(8,128)S(1)}, f32[1,1,16,2048]{3,2,1,0:T(8,128)S(1)}, f32[1,1,16,2048]{3,2,1,0:T(8,128)S(1)}, f32[1,1,16,204...) fusion(f32[1,5,16,2048]{3,2,1,0:T(8,128)S(1)} %slice.181, f32[1,8,16,2048]{3,2,1,0:T(8,128)} %copy-done.2, ...), kind=kLoop, calls=%fused_computation.102 | loop fusion | flops 917504 | bytes 2490368 | tf_op jit(solution)/shard_map/sub | solution.py:50
  207.7 1.9 fusion.55
  209.8 1.2 fusion.51
  211.6 1.1 copy-done.12
  212.8 0.7 constant_dynamic-update-slice_fusion
  (85 shorter events, 5.6 us)
Async XLA Ops:
  1.9 50.7 %collective-permute-start = (f32[1,4,16,2048]{3,2,1,0:T(8,128)}, f32[1,4,16,2048]{3,2,1,0:T(8,128)S(1)}, u32[]{:S(2)}, u32[]{:S(2)}) collective-permute-start(f32[1,4,16,2048]{3,2,1,0:T(8,128)} %slice.160), channel_id=1, source_target_pairs={{8,0},{10,2},{12,4},{14,6},{0,8},{2,10},{4,12},{6,14},{9,1},{11,3}... | collective-permute-start | bytes 1572872 | tf_op jit(solution)/shard_map/ppermute | solution.py:22
  8.2 110.8 %collective-permute-start.1 = (f32[1,8,16,2048]{3,2,1,0:T(8,128)}, f32[1,8,16,2048]{3,2,1,0:T(8,128)S(1)}, u32[]{:S(2)}, u32[]{:S(2)}) collective-permute-start(f32[1,8,16,2048]{3,2,1,0:T(8,128)} %slice.163), channel_id=1, source_target_pairs={{8,0},{10,2},{12,4},{14,6},{0,8},{2,10},{4,12},{6,14},{9,1},{11,3}... | collective-permute-start | bytes 3145736 | tf_op jit(solution)/shard_map/ppermute | solution.py:22
  33.2 9.6 %slice-start = ((s8[8388608]{0:T(1024)(128)(4,1)}), s8[4194304]{0:T(1024)(128)(4,1)S(1)}, s32[]{:S(2)}) async-start(s8[8388608]{0:T(1024)(128)(4,1)} %bitcast.155), calls=%async_computation.2 | async-start | bytes 8388608
  33.2 9.6 %slice-start.1 = ((s8[8388608]{0:T(1024)(128)(4,1)}), s8[4194304]{0:T(1024)(128)(4,1)S(1)}, s32[]{:S(2)}) async-start(s8[8388608]{0:T(1024)(128)(4,1)} %bitcast.155), calls=%async_computation.3 | async-start | bytes 8388608
  52.6 0.8 copy-start.4
  91.9 9.4 %copy-start = (f32[64,32,512]{2,1,0:T(8,128)S(1)}, f32[64,32,512]{2,1,0:T(8,128)}, u32[]{:S(2)}) copy-start(f32[64,32,512]{2,1,0:T(8,128)} %reshape_reshape.13) | copy-start | bytes 12582916
  110.2 8.8 %copy-start.1 = (f32[64,32,512]{2,1,0:T(8,128)S(1)}, f32[64,32,512]{2,1,0:T(8,128)}, u32[]{:S(2)}) copy-start(f32[64,32,512]{2,1,0:T(8,128)} %fusion.9) | copy-start | bytes 12582916
  119.0 4.0 %copy-start.2 = (f32[1,8,16,2048]{3,2,1,0:T(8,128)}, f32[1,8,16,2048]{3,2,1,0:T(8,128)S(1)}, u32[]{:S(2)}) copy-start(f32[1,8,16,2048]{3,2,1,0:T(8,128)S(1)} %collective-permute-done.1) | copy-start | bytes 3145732
  139.4 37.4 %collective-permute-start.2 = (f32[96,1024]{1,0:T(8,128)S(1)}, f32[96,1024]{1,0:T(8,128)S(1)}, u32[]{:S(2)}, u32[]{:S(2)}) collective-permute-start(f32[96,1024]{1,0:T(8,128)S(1)} %mul.1433), channel_id=1, source_target_pairs={{8,0},{10,2},{12,4},{14,6},{0,8},{2,10},{4,12},{6,14},{9,1},{11,3}... | collective-permute-start | bytes 1179656 | tf_op jit(solution)/shard_map/ppermute | solution.py:22
  141.8 53.2 %collective-permute-start.3 = (f32[96,1024]{1,0:T(8,128)S(1)}, f32[96,1024]{1,0:T(8,128)S(1)}, u32[]{:S(2)}, u32[]{:S(2)}) collective-permute-start(f32[96,1024]{1,0:T(8,128)S(1)} %mul.1433), channel_id=1, source_target_pairs={{10,0},{12,2},{14,4},{0,6},{2,8},{4,10},{6,12},{8,14},{11,1},{13,3... | collective-permute-start | bytes 1179656 | tf_op jit(solution)/shard_map/ppermute | solution.py:22
  144.3 50.9 %collective-permute-start.4 = (f32[96,1024]{1,0:T(8,128)S(1)}, f32[96,1024]{1,0:T(8,128)S(1)}, u32[]{:S(2)}, u32[]{:S(2)}) collective-permute-start(f32[96,1024]{1,0:T(8,128)S(1)} %mul.1433), channel_id=1, source_target_pairs={{12,0},{14,2},{0,4},{2,6},{4,8},{6,10},{8,12},{10,14},{13,1},{15,3... | collective-permute-start | bytes 1179656 | tf_op jit(solution)/shard_map/ppermute | solution.py:22
  144.3 51.1 %collective-permute-start.5 = (f32[96,1024]{1,0:T(8,128)S(1)}, f32[96,1024]{1,0:T(8,128)S(1)}, u32[]{:S(2)}, u32[]{:S(2)}) collective-permute-start(f32[96,1024]{1,0:T(8,128)S(1)} %mul.1433), channel_id=1, source_target_pairs={{14,0},{0,2},{2,4},{4,6},{6,8},{8,10},{10,12},{12,14},{15,1},{1,3}... | collective-permute-start | bytes 1179656 | tf_op jit(solution)/shard_map/ppermute | solution.py:22
  195.6 0.7 copy-start.11
  195.9 0.7 copy-start.10
  200.9 1.4 copy-start.9
  205.5 4.3 %copy-start.5 = (f32[1,4,16,2048]{3,2,1,0:T(8,128)S(1)}, f32[1,4,16,2048]{3,2,1,0:T(8,128)}, u32[]{:S(2)}) copy-start(f32[1,4,16,2048]{3,2,1,0:T(8,128)} %copy-done.4) | copy-start | bytes 1572868
  209.7 1.4 copy-start.3
  209.7 1.4 copy-start.6
  209.7 1.4 copy-start.7
  209.7 1.5 copy-start.8
  211.6 1.1 copy-start.12
